TPU v7x, 32 devices: a whole 2x2x4 slice. The times are simulated.
32 devices in a mesh: groups: 2 (over y), prompt: 4 (over z), enc: 4 (over x, core).
Axes of the slice: x: 2, y: 2, z: 4, core: 2. Of those that a mesh axis runs over, the one named last changes fastest.
Arguments:
- embed: bfloat16 [8192, 256], P(('groups', 'prompt', 'enc')), parts along dimension 0, may hold values from -4000 to 4000
- coords: int32 [64, 6], P(('groups', 'prompt')), parts along dimension 0, may hold values from 0 to 1023
- targets: int32 [64], P(('groups', 'prompt')), parts along dimension 0, may hold values from 0 to 7
- counts: int32 [4], replicated, may hold values from 1 to 8, 16 in all
- labels: int32 [512, 256], P('groups'), parts along dimension 0, may hold values from 0 to 7
- type_embed: float32 [4, 256], replicated, may hold values from -5 to 5
- fourier: float32 [2, 128], replicated, may hold values from -5 to 5
- wq_t: bfloat16 [256, 128], replicated, may hold values from -0.375 to 0.375
- wk_t: bfloat16 [256, 128], replicated, may hold values from -0.375 to 0.375
- wv_t: bfloat16 [256, 128], replicated, may hold values from -0.375 to 0.375
- wo_t: bfloat16 [128, 256], replicated, may hold values from -0.5 to 0.5
- wq_i: bfloat16 [256, 128], replicated, may hold values from -0.375 to 0.375
- wk_i: bfloat16 [256, 128], replicated, may hold values from -0.375 to 0.375
- wv_i: bfloat16 [256, 128], replicated, may hold values from -0.375 to 0.375
- wo_i: bfloat16 [128, 256], replicated, may hold values from -0.5 to 0.5
- gain_one: float32 [256], replicated, may hold values from 0.1 to 1.9
- gain_two: float32 [256], replicated, may hold values from 0.1 to 1.9
- gain_three: float32 [64], replicated, may hold values from 0.1 to 1.9
- up_one: bfloat16 [256, 256], replicated, may hold values from -0.375 to 0.375
- second_upsample_weight: bfloat16 [64, 128], replicated, may hold values from -0.75 to 0.75
- hyper_one: bfloat16 [256, 256], replicated, may hold values from -0.375 to 0.375
- hyper_two: bfloat16 [256, 32], replicated, may hold values from -0.375 to 0.375
Outputs:
- grad_embed: float32 [8192, 256], P(('groups', 'prompt', 'enc')), parts along dimension 0
There are 2 independent parts, one for each index of `groups`. A program takes and returns all parts, laid end to end along the dimension named above; an argument that names none is the same for every part. Nothing has to cross between parts.
Inputs may be any that keep to these rules, and one draw needn't show every extreme that they name: Prompt index p has counts[p] live prompts, in its first slots; the counts sum to 16 and the largest is 8.
All inputs are finite; a program needn't handle non-finite values.
Results may differ from a plain program's by a relative error of at most 0.0035.
Values may be sent and summed in bfloat16 or wider, within the bound.
No kernel may reach another device: no remote copies, remote signals or barrier semaphores. Data moves between devices by JAX's collectives and lax.ppermute only.
A program may use at most 128 MiB of HBM per device.

v0:
```python
import math
import jax
import jax.numpy as jnp
from jax import lax
from jax.sharding import PartitionSpec as P

HEADS = 8
HD = 16
IMG = 1024
highest_value = lax.Precision.HIGHEST
epsilon = 1e-05


def joined(array, axis, combine):
    everything = jax.tree.map(lambda part: lax.all_gather(part, axis), array)
    leading = jax.tree.map(lambda part: part[0], everything)

    def step(k, so_far):
        return combine(so_far, jax.tree.map(lambda part: part[k], everything))

    return lax.fori_loop(1, lax.axis_size(axis), step, leading)


def layer_norm(values, gain):
    centered = values - jnp.mean(values, axis=-1, keepdims=True)
    variance = jnp.mean(centered * centered, axis=-1, keepdims=True)
    return centered * lax.rsqrt(variance + epsilon) * gain


def fourier_code(pixel_pair, fourier):
    scaled = 2.0 * ((pixel_pair.astype(jnp.float32) + 0.5) / IMG) - 1.0
    angles = 2.0 * math.pi * jnp.dot(scaled, fourier, precision=highest_value)
    return jnp.concatenate([jnp.sin(angles), jnp.cos(angles)], axis=-1)


def prompt_tokens(corner_rows, type_embed, fourier):
    point_code = fourier_code(corner_rows[..., 0:2], fourier) + type_embed[1]
    first_code = fourier_code(corner_rows[..., 2:4], fourier) + type_embed[2]
    second_code = fourier_code(corner_rows[..., 4:6], fourier) + type_embed[3]
    output_token = jnp.broadcast_to(type_embed[0], point_code.shape)
    return jnp.stack([output_token, point_code, first_code, second_code], axis=-2)


def token_pixel_scores(labels):
    side = labels.shape[0] // 4
    grid_view = labels.reshape(side, 2, 2, side, 2, 2)
    grid_view = jnp.transpose(grid_view, (0, 3, 1, 4, 2, 5))
    return grid_view.reshape(side * side, 4, 4)


def combine_parts(first, second_result):
    top_first, first_running_total, accum_first = first
    top_second, total_second, accum_second = second_result
    top_both = jnp.maximum(top_first, top_second)
    factor_first = jnp.exp(top_first - top_both)
    factor_second = jnp.exp(top_second - top_both)
    total_both = first_running_total * factor_first + total_second * factor_second
    accum_both = accum_first * factor_first[..., None] + accum_second * factor_second[..., None]
    return (top_both, total_both, accum_both)


def image_side(query_image, image_float, tokens_one, truth, live_flag, side_weights):
    wk_i, wv_i, wo_i, gain_two, up_one, gain_three, second_upsample_weight, hyper_one, hyper_two = (
        side_weights
    )
    head_scale = HD ** (-0.5)
    row_count = query_image.shape[0]
    token_keys = jnp.dot(tokens_one, wk_i.astype(jnp.float32), precision=highest_value).reshape(
        -1, HEADS, HD
    )
    token_values = jnp.dot(tokens_one, wv_i.astype(jnp.float32), precision=highest_value).reshape(
        -1, HEADS, HD
    )
    scores = (
        jnp.einsum(
            "jhd,rhd->jhr",
            query_image.reshape(row_count, HEADS, HD),
            token_keys,
            precision=highest_value,
        )
        * head_scale
    )
    attention = jax.nn.softmax(scores, axis=-1)
    mixed = (
        jnp.einsum("jhr,rhd->jhd", attention, token_values, precision=highest_value)
        .reshape(row_count, -1)
        .astype(jnp.bfloat16)
    )
    update = jnp.dot(mixed, wo_i, preferred_element_type=jnp.float32)
    image_one = layer_norm(image_float + update, gain_two).astype(jnp.bfloat16)
    lifted = jnp.dot(image_one, up_one, preferred_element_type=jnp.float32).reshape(
        row_count, 4, -1
    )
    first_activation = jax.nn.gelu(layer_norm(lifted, gain_three), approximate=False).astype(
        jnp.bfloat16
    )
    second_result = jnp.einsum(
        "oij,jp->oip", first_activation, second_upsample_weight, preferred_element_type=jnp.float32
    )
    features = jax.nn.gelu(second_result, approximate=False).reshape(row_count, 4, 4, -1)
    hidden = jax.nn.relu(
        jnp.dot(tokens_one[0], hyper_one.astype(jnp.float32), precision=highest_value)
    )
    hyper = jnp.dot(hidden, hyper_two.astype(jnp.float32), precision=highest_value)
    logits = jnp.einsum("tasc,c->tas", features, hyper, precision=highest_value)
    losses = jax.nn.softplus(logits) - truth * logits
    return jnp.sum(losses) * live_flag * 0.25


def on_device(
    embed,
    coords,
    targets,
    counts,
    labels,
    type_embed,
    fourier,
    wq_t,
    wk_t,
    wv_t,
    wo_t,
    wq_i,
    wk_i,
    wv_i,
    wo_i,
    gain_one,
    gain_two,
    gain_three,
    up_one,
    second_upsample_weight,
    hyper_one,
    hyper_two,
):
    prompt_count = lax.axis_size("prompt")
    enc_count = lax.axis_size("enc")
    prompt_place = lax.axis_index("prompt")
    enc_place = lax.axis_index("enc")
    block_rows = embed.shape[0]
    slot_count = coords.shape[0]
    head_scale = HD ** (-0.5)
    image = lax.all_gather(embed, "prompt", axis=0, tiled=True)
    image_float = image.astype(jnp.float32)
    key_image = jnp.dot(image, wk_t, preferred_element_type=jnp.float32)
    value_image = jnp.dot(image, wv_t, preferred_element_type=jnp.float32)
    query_image = jnp.dot(image, wq_i, preferred_element_type=jnp.float32)
    local_rows = image.shape[0]
    pixel_all = token_pixel_scores(labels).reshape(prompt_count, enc_count, block_rows, 4, 4)
    own_pixels = lax.dynamic_index_in_dim(pixel_all, enc_place, axis=1, keepdims=False).reshape(
        local_rows, 4, 4
    )
    own_count = jnp.take(counts, prompt_place)
    live_flags = (jnp.arange(slot_count, dtype=jnp.int32) < own_count).astype(jnp.float32)
    tokens_zero = prompt_tokens(coords, type_embed, fourier)
    prompt_number = tokens_zero.shape[0]
    flat_tokens = tokens_zero.reshape(prompt_number * 4, -1)
    queries = jnp.dot(flat_tokens, wq_t.astype(jnp.float32), precision=highest_value).reshape(
        -1, HEADS, HD
    )
    key_heads = key_image.reshape(local_rows, HEADS, HD)
    value_heads = value_image.reshape(local_rows, HEADS, HD)
    scores = jnp.einsum("rhd,jhd->rhj", queries, key_heads, precision=highest_value) * head_scale
    local_top = jnp.max(scores, axis=-1)
    shifted = jnp.exp(scores - local_top[..., None])
    local_total = jnp.sum(shifted, axis=-1)
    local_accum = jnp.einsum("rhj,jhd->rhd", shifted, value_heads, precision=highest_value)
    global_top, global_total, global_accum = joined(
        (local_top, local_total, local_accum), "enc", combine_parts
    )
    gathered = global_accum / global_total[..., None]
    wo_t_float = wo_t.astype(jnp.float32)
    update = jnp.dot(gathered.reshape(prompt_number * 4, -1), wo_t_float, precision=highest_value)

    def token_norm(values):
        return layer_norm(values, gain_one)

    tokens_one, norm_pull = jax.vjp(token_norm, flat_tokens + update)
    side_weights = (
        wk_i,
        wv_i,
        wo_i,
        gain_two,
        up_one,
        gain_three,
        second_upsample_weight,
        hyper_one,
        hyper_two,
    )

    def single_prompt(carry, inputs):
        tokens_row, target, live_flag = inputs
        truth = (own_pixels == target).astype(jnp.float32)

        def loss_of(query_arg, image_arg, tokens_arg):
            return image_side(query_arg, image_arg, tokens_arg, truth, live_flag, side_weights)

        _, pullback = jax.vjp(loss_of, query_image, image_float, tokens_row)
        d_query, d_image, d_tokens = pullback(jnp.ones((), jnp.float32))
        return ((carry[0] + d_query, carry[1] + d_image), d_tokens)

    initial = (jnp.zeros_like(query_image), jnp.zeros_like(image_float))
    sums, token_parts = lax.scan(
        single_prompt, initial, (tokens_one.reshape(prompt_number, 4, -1), targets, live_flags)
    )
    query_grad, image_grad = sums
    token_grad = lax.psum(token_parts, "enc")
    (d_residual,) = norm_pull(token_grad.reshape(prompt_number * 4, -1))
    d_gathered = jnp.dot(d_residual, wo_t_float.T, precision=highest_value).reshape(-1, HEADS, HD)
    probs = jnp.exp(scores - global_top[..., None]) / global_total[..., None]
    d_probs = jnp.einsum("rhd,jhd->rhj", d_gathered, value_heads, precision=highest_value)
    delta_term = jnp.sum(d_gathered * gathered, axis=-1)
    d_scores = probs * (d_probs - delta_term[..., None]) * head_scale
    key_grad = jnp.einsum("rhj,rhd->jhd", d_scores, queries, precision=highest_value).reshape(
        local_rows, -1
    )
    value_grad = jnp.einsum("rhj,rhd->jhd", probs, d_gathered, precision=highest_value).reshape(
        local_rows, -1
    )
    wq_i_float = wq_i.astype(jnp.float32)
    wk_t_float = wk_t.astype(jnp.float32)
    wv_t_float = wv_t.astype(jnp.float32)
    result = image_grad
    result = result + jnp.dot(query_grad, wq_i_float.T, precision=highest_value)
    result = result + jnp.dot(key_grad, wk_t_float.T, precision=highest_value)
    result = result + jnp.dot(value_grad, wv_t_float.T, precision=highest_value)
    summed = lax.psum(result, "prompt")
    grad_embed = lax.dynamic_slice_in_dim(summed, prompt_place * block_rows, block_rows, 0)
    return grad_embed


def solution(mesh):
    in_specs = (
        P(("groups", "prompt", "enc"), None),
        P(("groups", "prompt"), None),
        P(("groups", "prompt")),
        P(),
        P("groups", None),
        P(),
        P(),
        P(),
        P(),
        P(),
        P(),
        P(),
        P(),
        P(),
        P(),
        P(),
        P(),
        P(),
        P(),
        P(),
        P(),
        P(),
    )
    out_specs = P(("groups", "prompt", "enc"), None)
    return jax.shard_map(
        on_device, mesh=mesh, in_specs=in_specs, out_specs=out_specs, check_vma=False
    )
```

profile of v0, /device:TPU:0, one launch (start us, length us, event | category | flops | bytes accessed | tf_op | source)
XLA Modules:
  0.0 566.2 jit_solution(3963014833679820841)
XLA Ops:
  12.3 17.4 %all_gather.21 = bf16[1024,256]{0,1:T(8,128)(2,1)S(1)} all-gather(bf16[256,256]{0,1:T(8,128)(2,1)S(1)} %copy.50), channel_id=1, replica_groups=mesh['groups'=2,'prompt'=4,'enc'=4] {'prompt'}, dimensions={0}, use_global_device_ids=true | all-gather | bytes 655360 | tf_op jit(solution)/shard_map/all_gather | solution.py:141
  33.9 7.2 %all-gather.2 = f32[128,8,16]{2,1,0:T(8,128)S(1)} all-gather(f32[32,8,16]{2,1,0:T(8,128)S(1)} %copy.52), channel_id=4, replica_groups=mesh['groups'=2,'prompt'=4,'enc'=4] {'enc'}, dimensions={0}, use_global_device_ids=true | all-gather | bytes 81920 | tf_op jit(solution)/shard_map/all_gather | solution.py:15
  41.4 5.2 all-gather.4
  46.6 5.2 all-gather.3
  55.4 27.0 %reshape.331 = s32[64,2,2,64,2,2]{5,4,3,2,1,0:T(2,128)} reshape(s32[256,256]{1,0:T(8,128)S(1)} %copy-done.55) | data formatting | bytes 524288 | tf_op jit(solution)/shard_map/reshape | solution.py:46
  82.4 20.9 %copy.55 = s32[64,64,2,2,2,2]{1,0,5,4,3,2:T(8,128)S(1)} copy(s32[64,64,2,2,2,2]{5,3,1,4,2,0:T(2,128)} %bitcast.446) | data formatting | bytes 524288 | tf_op jit(solution)/shard_map/transpose | solution.py:47
  105.7 374.7 %while.36 = (s32[]{:T(128)}, f32[1024,128]{0,1:T(8,128)}, f32[1024,256]{0,1:T(8,128)}, f32[8,4,256]{2,1,0:T(4,128)}, f32[8,4,256]{2,1,0:T(4,128)}, /*index=5*/bf...) while((s32[]{:T(128)}, f32[1024,128]{0,1:T(8,128)}, ...), condition=%wide.region_18.19_spmd.clone, body=%wide.region_6.18_spmd.clone.sunk | while | flops 692868864 | bytes 118107712 | solution.py:201
  112.7 3.8 fusion.345
  116.6 5.5 multiply_multiply_fusion.19
  129.5 2.7 fusion.348
  132.2 3.6 multiply_reduce_fusion.13
  158.6 3.8 fusion.345
  162.5 5.5 multiply_multiply_fusion.19
  175.4 2.7 fusion.348
  178.0 3.6 multiply_reduce_fusion.13
  196.5 1.9 bitcast_add_fusion.2
  205.6 3.8 fusion.345
  209.4 5.5 multiply_multiply_fusion.19
  222.3 2.7 fusion.348
  225.0 3.6 multiply_reduce_fusion.13
  243.5 1.9 bitcast_add_fusion.2
  252.5 3.8 fusion.345
  256.3 5.5 multiply_multiply_fusion.19
  269.3 2.7 fusion.348
  271.9 3.6 multiply_reduce_fusion.13
  290.4 1.9 bitcast_add_fusion.2
  299.4 3.8 fusion.345
  303.3 5.5 multiply_multiply_fusion.19
  316.2 2.7 fusion.348
  318.9 3.6 multiply_reduce_fusion.13
  337.4 1.9 bitcast_add_fusion.2
  346.4 3.8 fusion.345
  350.2 5.5 multiply_multiply_fusion.19
  363.2 2.7 fusion.348
  365.8 3.6 multiply_reduce_fusion.13
  384.3 1.9 bitcast_add_fusion.2
  393.3 3.8 fusion.345
  397.2 5.5 multiply_multiply_fusion.19
  410.1 2.7 fusion.348
  412.8 3.6 multiply_reduce_fusion.13
  431.3 1.9 bitcast_add_fusion.2
  440.3 3.8 fusion.345
  444.1 5.5 multiply_multiply_fusion.19
  457.0 2.7 fusion.348
  459.7 3.6 multiply_reduce_fusion.13
  481.2 10.9 %psum.14 = f32[32,256]{1,0:T(8,128)S(1)} all-reduce(f32[32,256]{1,0:T(8,128)S(1)} %reshape.333), channel_id=1, replica_groups=mesh['groups'=2,'prompt'=4,'enc'=4] {'enc'}, use_global_device_ids=true, to_apply=%region_19.20 | all-reduce | flops 8192 | bytes 65536 | tf_op jit(solution)/shard_map/psum | solution.py:205
  496.0 2.1 fusion.118
  504.3 53.4 %all-reduce.3.cloned.1.call-done = f32[1024,256]{1,0:T(8,128)} async-done(((f32[1024,256]{1,0:T(8,128)}), f32[1024,256]{1,0:T(8,128)}) %all-reduce.3.cloned.1.call-update) | async-done | bytes 1048592 | tf_op jit(solution)/shard_map/psum | solution.py:225
  (1284 shorter events, 255.2 us)
Async XLA Ops:
  6.5 98.0 %copy-start = (bf16[256,128]{1,0:T(8,128)(2,1)S(1)}, bf16[256,128]{1,0:T(8,128)(2,1)}, u32[]{:S(2)}) copy-start(bf16[256,128]{1,0:T(8,128)(2,1)} %param.37) | copy-start | bytes 196612
  6.5 23.2 %copy-start.57 = (bf16[256,128]{1,0:T(8,128)(2,1)S(1)}, bf16[256,128]{1,0:T(8,128)(2,1)}, u32[]{:S(2)}) copy-start(bf16[256,128]{1,0:T(8,128)(2,1)} %param.34) | copy-start | bytes 196612
  6.5 23.5 %copy-start.59 = (bf16[256,128]{1,0:T(8,128)(2,1)S(1)}, bf16[256,128]{1,0:T(8,128)(2,1)}, u32[]{:S(2)}) copy-start(bf16[256,128]{1,0:T(8,128)(2,1)} %param.35) | copy-start | bytes 196612
  6.5 551.2 %all-reduce.3.cloned.1.call-start = ((), (), s32[]{:S(2)}) async-start(), calls=%async_computation | async-start | bytes 2097152 | tf_op jit(solution)/shard_map/psum | solution.py:225
  33.8 18.3 %copy-start.56 = (bf16[128,256]{1,0:T(8,128)(2,1)S(1)}, bf16[128,256]{1,0:T(8,128)(2,1)}, u32[]{:S(2)}) copy-start(bf16[128,256]{1,0:T(8,128)(2,1)} %param.36) | copy-start | bytes 196612
  33.8 19.2 %copy-start.70 = (f32[256]{0:T(256)S(1)}, f32[256]{0:T(256)}, u32[]{:S(2)}) copy-start(f32[256]{0:T(256)} %param.41) | copy-start | bytes 3076
  33.8 19.9 %copy-start.74 = (s32[4]{0:T(128)S(1)}, s32[4]{0:T(128)}, u32[]{:S(2)}) copy-start(s32[4]{0:T(128)} %param.29) | copy-start | bytes 52
  33.8 21.6 %copy-start.55 = (s32[256,256]{1,0:T(8,128)S(1)}, s32[256,256]{1,0:T(8,128)}, u32[]{:S(2)}) copy-start(s32[256,256]{1,0:T(8,128)} %param.30) | copy-start | bytes 786436
  52.0 30.4 %copy-start.63 = (f32[32,8]{0,1:T(8,128)}, f32[32,8]{0,1:T(8,128)S(1)}, u32[]{:S(2)}) copy-start(f32[32,8]{0,1:T(8,128)S(1)} %get-tuple-element.283) | copy-start | bytes 3076
  52.0 30.4 %copy-start.65 = (f32[32,8]{0,1:T(8,128)}, f32[32,8]{0,1:T(8,128)S(1)}, u32[]{:S(2)}) copy-start(f32[32,8]{0,1:T(8,128)S(1)} %get-tuple-element.286) | copy-start | bytes 3076
  52.0 30.4 %copy-start.52 = (f32[32,8,16]{0,2,1:T(8,128)}, f32[32,8,16]{0,2,1:T(8,128)S(1)}, u32[]{:S(2)}) copy-start(f32[32,8,16]{0,2,1:T(8,128)S(1)} %broadcast_divide_fusion) | copy-start | bytes 49156
  52.4 30.0 %copy-start.71 = (f32[32]{0:T(128)}, f32[32]{0:T(128)S(1)}, u32[]{:S(2)}) copy-start(f32[32]{0:T(128)S(1)} %broadcast_multiply_fusion.3) | copy-start | bytes 388
  52.6 29.8 %copy-start.73 = (f32[32]{0:T(128)}, f32[32]{0:T(128)S(1)}, u32[]{:S(2)}) copy-start(f32[32]{0:T(128)S(1)} %multiply_reduce_fusion.6) | copy-start | bytes 388
  53.0 29.5 %copy-start.72 = (f32[32]{0:T(128)}, f32[32]{0:T(128)S(1)}, u32[]{:S(2)}) copy-start(f32[32]{0:T(128)S(1)} %fusion.146) | copy-start | bytes 388
  105.7 5.0 copy-start.22
  116.5 5.6 copy-start.5
  116.5 5.6 copy-start.18
  116.5 6.4 %copy-start.53 = (bf16[256,32]{0,1:T(8,128)(2,1)S(1)}, bf16[256,32]{0,1:T(8,128)(2,1)}, u32[]{:S(2)}) copy-start(bf16[256,32]{0,1:T(8,128)(2,1)} %get-tuple-element.825) | copy-start | bytes 49156 | tf_op jit(solution)/shard_map/while
  141.7 6.0 %copy-start.4 = (f32[1024,256]{0,1:T(8,128)S(1)}, f32[1024,256]{0,1:T(8,128)}, u32[]{:S(2)}) copy-start(f32[1024,256]{0,1:T(8,128)} %copy-done.3) | copy-start | bytes 3145732 | tf_op jit(solution)/shard_map/while
  162.4 5.6 copy-start.5
  162.4 5.6 copy-start.18
  162.4 6.4 %copy-start.53 = (bf16[256,32]{0,1:T(8,128)(2,1)S(1)}, bf16[256,32]{0,1:T(8,128)(2,1)}, u32[]{:S(2)}) copy-start(bf16[256,32]{0,1:T(8,128)(2,1)} %get-tuple-element.825) | copy-start | bytes 49156 | tf_op jit(solution)/shard_map/while
  187.5 6.0 %copy-start.4 = (f32[1024,256]{0,1:T(8,128)S(1)}, f32[1024,256]{0,1:T(8,128)}, u32[]{:S(2)}) copy-start(f32[1024,256]{0,1:T(8,128)} %copy-done.3) | copy-start | bytes 3145732 | tf_op jit(solution)/shard_map/while
  209.4 5.6 copy-start.5
  209.4 5.6 copy-start.18
  209.4 6.5 %copy-start.53 = (bf16[256,32]{0,1:T(8,128)(2,1)S(1)}, bf16[256,32]{0,1:T(8,128)(2,1)}, u32[]{:S(2)}) copy-start(bf16[256,32]{0,1:T(8,128)(2,1)} %get-tuple-element.825) | copy-start | bytes 49156 | tf_op jit(solution)/shard_map/while
  234.5 6.0 %copy-start.4 = (f32[1024,256]{0,1:T(8,128)S(1)}, f32[1024,256]{0,1:T(8,128)}, u32[]{:S(2)}) copy-start(f32[1024,256]{0,1:T(8,128)} %copy-done.3) | copy-start | bytes 3145732 | tf_op jit(solution)/shard_map/while
  256.3 5.6 copy-start.5
  256.3 5.6 copy-start.18
  256.3 6.5 %copy-start.53 = (bf16[256,32]{0,1:T(8,128)(2,1)S(1)}, bf16[256,32]{0,1:T(8,128)(2,1)}, u32[]{:S(2)}) copy-start(bf16[256,32]{0,1:T(8,128)(2,1)} %get-tuple-element.825) | copy-start | bytes 49156 | tf_op jit(solution)/shard_map/while
  281.5 6.0 %copy-start.4 = (f32[1024,256]{0,1:T(8,128)S(1)}, f32[1024,256]{0,1:T(8,128)}, u32[]{:S(2)}) copy-start(f32[1024,256]{0,1:T(8,128)} %copy-done.3) | copy-start | bytes 3145732 | tf_op jit(solution)/shard_map/while
  303.3 5.6 copy-start.5
  303.3 5.6 copy-start.18
  303.3 6.5 %copy-start.53 = (bf16[256,32]{0,1:T(8,128)(2,1)S(1)}, bf16[256,32]{0,1:T(8,128)(2,1)}, u32[]{:S(2)}) copy-start(bf16[256,32]{0,1:T(8,128)(2,1)} %get-tuple-element.825) | copy-start | bytes 49156 | tf_op jit(solution)/shard_map/while
  328.4 6.0 %copy-start.4 = (f32[1024,256]{0,1:T(8,128)S(1)}, f32[1024,256]{0,1:T(8,128)}, u32[]{:S(2)}) copy-start(f32[1024,256]{0,1:T(8,128)} %copy-done.3) | copy-start | bytes 3145732 | tf_op jit(solution)/shard_map/while
  339.3 4.9 copy-start.7
  350.2 5.6 copy-start.5
  350.2 5.6 copy-start.18
  350.2 6.5 %copy-start.53 = (bf16[256,32]{0,1:T(8,128)(2,1)S(1)}, bf16[256,32]{0,1:T(8,128)(2,1)}, u32[]{:S(2)}) copy-start(bf16[256,32]{0,1:T(8,128)(2,1)} %get-tuple-element.825) | copy-start | bytes 49156 | tf_op jit(solution)/shard_map/while
  375.3 6.0 %copy-start.4 = (f32[1024,256]{0,1:T(8,128)S(1)}, f32[1024,256]{0,1:T(8,128)}, u32[]{:S(2)}) copy-start(f32[1024,256]{0,1:T(8,128)} %copy-done.3) | copy-start | bytes 3145732 | tf_op jit(solution)/shard_map/while
  397.2 5.6 copy-start.5
  397.2 5.6 copy-start.18
  397.2 6.4 %copy-start.53 = (bf16[256,32]{0,1:T(8,128)(2,1)S(1)}, bf16[256,32]{0,1:T(8,128)(2,1)}, u32[]{:S(2)}) copy-start(bf16[256,32]{0,1:T(8,128)(2,1)} %get-tuple-element.825) | copy-start | bytes 49156 | tf_op jit(solution)/shard_map/while
  422.3 6.0 %copy-start.4 = (f32[1024,256]{0,1:T(8,128)S(1)}, f32[1024,256]{0,1:T(8,128)}, u32[]{:S(2)}) copy-start(f32[1024,256]{0,1:T(8,128)} %copy-done.3) | copy-start | bytes 3145732 | tf_op jit(solution)/shard_map/while
  444.1 5.6 copy-start.5
  444.1 5.6 copy-start.18
  444.1 6.4 %copy-start.53 = (bf16[256,32]{0,1:T(8,128)(2,1)S(1)}, bf16[256,32]{0,1:T(8,128)(2,1)}, u32[]{:S(2)}) copy-start(bf16[256,32]{0,1:T(8,128)(2,1)} %get-tuple-element.825) | copy-start | bytes 49156 | tf_op jit(solution)/shard_map/while
  469.2 6.0 %copy-start.4 = (f32[1024,256]{0,1:T(8,128)S(1)}, f32[1024,256]{0,1:T(8,128)}, u32[]{:S(2)}) copy-start(f32[1024,256]{0,1:T(8,128)} %copy-done.3) | copy-start | bytes 3145732 | tf_op jit(solution)/shard_map/while
  (373 other events, 937.8 us)
Sparse Core Ops, SparseCore 0:
  504.4 53.2 all-reduce.2
where the time goes:
time: 573 us; the launch traced here: 566 us
  matrix products  223 us (39%)
  other arithmetic  124 us (22%)
  local copies, waits for them, and re-layouts  95 us (17%)
  waiting for transfers between devices  53.4 us (9%)
  blocking collectives  45.8 us (8%)
  between operations  14.6 us (3%)
  loops' own time  11.1 us (2%)
    dot_general x16, matrix products, image_side(): jnp.einsum('oij,jp->oip', first_activation, second_upsample_weight, prefe...  59.2 us
    psum x1, waiting for transfers between devices, on_device(): summed = lax.psum(result, 'prompt')  53.4 us
    mul x8, other arithmetic, image_side(): jax.nn.gelu(second_result, approximate=False).reshape(row_count, 4, 4, -1)  44.4 us
    dot_general x16, matrix products, image_side(): logits = jnp.einsum('tasc,c->tas', features, hyper, precision=highest_value)  28.8 us
    reshape x1, local copies, waits for them, and re-layouts, token_pixel_scores(): grid_view = labels.reshape(side, 2, 2, side, 2, 2)  27 us
    dot_general x24, matrix products, image_side(): jnp.einsum('jhd,rhd->jhr', query_image.reshape(row_count, HEADS, HD), tok...  24.1 us
    dot_general x16, matrix products, image_side(): jnp.dot(tokens_one, wk_i.astype(jnp.float32), precision=highest_value)  23 us
    add x16, other arithmetic, single_prompt(): return ((carry[0] + d_query, carry[1] + d_image), d_tokens)  22.7 us
  transfers between devices with their start and end apart: 1, of which 1 were waited for; matrix products, arithmetic and copies ran while one was open for 0% of the time, Pallas kernels for 0%

commit v1 on v0

--- a/solution.py
+++ b/solution.py
@@ -131,6 +131,11 @@
     hyper_one,
     hyper_two,
 ):
+
+    def review_row_on_mesh(a0, peer_axis):
+        long_array = lax.all_gather(a0, peer_axis)
+        return jnp.sum(long_array, 0)
+
     prompt_count = lax.axis_size("prompt")
     enc_count = lax.axis_size("enc")
     prompt_place = lax.axis_index("prompt")
@@ -222,7 +227,7 @@
     result = result + jnp.dot(query_grad, wq_i_float.T, precision=highest_value)
     result = result + jnp.dot(key_grad, wk_t_float.T, precision=highest_value)
     result = result + jnp.dot(value_grad, wv_t_float.T, precision=highest_value)
-    summed = lax.psum(result, "prompt")
+    summed = review_row_on_mesh(result, "prompt")
     grad_embed = lax.dynamic_slice_in_dim(summed, prompt_place * block_rows, block_rows, 0)
     return grad_embed
 

time: 573 us -> 603 us (1.052)
  waiting for transfers between devices: 53.4 us -> 82.4 us
    all_gather x0 -> x1, waiting for transfers between devices: none -> 82.4 us  [review_row_on_mesh(): long_array = lax.all_gather(a0, peer_axis)]
    psum x1 -> x0, waiting for transfers between devices: 53.4 us -> none  [on_device(): summed = lax.psum(result, 'prompt')]
where the time goes in v1:
time: 603 us; the launch traced here: 597 us
  matrix products  223 us (37%)
  other arithmetic  126 us (21%)
  local copies, waits for them, and re-layouts  94 us (16%)
  waiting for transfers between devices  82.4 us (14%)
  blocking collectives  45.8 us (8%)
  between operations  14.6 us (2%)
  loops' own time  11.1 us (2%)
    all_gather x1, waiting for transfers between devices, review_row_on_mesh(): long_array = lax.all_gather(a0, peer_axis)  82.4 us
    dot_general x16, matrix products, image_side(): jnp.einsum('oij,jp->oip', first_activation, second_upsample_weight, prefe...  59.2 us
    mul x8, other arithmetic, image_side(): jax.nn.gelu(second_result, approximate=False).reshape(row_count, 4, 4, -1)  44.4 us
    dot_general x16, matrix products, image_side(): logits = jnp.einsum('tasc,c->tas', features, hyper, precision=highest_value)  28.8 us
    reshape x1, local copies, waits for them, and re-layouts, token_pixel_scores(): grid_view = labels.reshape(side, 2, 2, side, 2, 2)  27 us
    dot_general x24, matrix products, image_side(): jnp.einsum('jhd,rhd->jhr', query_image.reshape(row_count, HEADS, HD), tok...  24.1 us
    dot_general x16, matrix products, image_side(): jnp.dot(tokens_one, wk_i.astype(jnp.float32), precision=highest_value)  23 us
    add x16, other arithmetic, single_prompt(): return ((carry[0] + d_query, carry[1] + d_image), d_tokens)  22.7 us
  transfers between devices with their start and end apart: 1, of which 1 were waited for; matrix products, arithmetic and copies ran while one was open for 0% of the time, Pallas kernels for 0%

profile of v1, /device:TPU:0, one launch (start us, length us, event | category | flops | bytes accessed | tf_op | source)
XLA Modules:
  0.0 596.9 jit_solution(15863343824143602529)
XLA Ops:
  12.3 17.4 %all_gather.27 = bf16[1024,256]{0,1:T(8,128)(2,1)S(1)} all-gather(bf16[256,256]{0,1:T(8,128)(2,1)S(1)} %copy.50), channel_id=1, replica_groups=mesh['groups'=2,'prompt'=4,'enc'=4] {'prompt'}, dimensions={0}, use_global_device_ids=true | all-gather | bytes 655360 | tf_op jit(solution)/shard_map/all_gather | solution.py:146
  33.9 7.2 %all-gather.2 = f32[128,8,16]{2,1,0:T(8,128)S(1)} all-gather(f32[32,8,16]{2,1,0:T(8,128)S(1)} %copy.52), channel_id=4, replica_groups=mesh['groups'=2,'prompt'=4,'enc'=4] {'enc'}, dimensions={0}, use_global_device_ids=true | all-gather | bytes 81920 | tf_op jit(solution)/shard_map/all_gather | solution.py:15
  41.4 5.2 all-gather.5
  46.6 5.2 all-gather.4
  55.4 27.0 %reshape.331 = s32[64,2,2,64,2,2]{5,4,3,2,1,0:T(2,128)} reshape(s32[256,256]{1,0:T(8,128)S(1)} %copy-done.55) | data formatting | bytes 524288 | tf_op jit(solution)/shard_map/reshape | solution.py:46
  82.4 20.9 %copy.55 = s32[64,64,2,2,2,2]{1,0,5,4,3,2:T(8,128)S(1)} copy(s32[64,64,2,2,2,2]{5,3,1,4,2,0:T(2,128)} %bitcast.447) | data formatting | bytes 524288 | tf_op jit(solution)/shard_map/transpose | solution.py:47
  105.7 374.7 %while.36 = (s32[]{:T(128)}, f32[1024,128]{0,1:T(8,128)}, f32[1024,256]{0,1:T(8,128)}, f32[8,4,256]{2,1,0:T(4,128)}, f32[8,4,256]{2,1,0:T(4,128)}, /*index=5*/bf...) while((s32[]{:T(128)}, f32[1024,128]{0,1:T(8,128)}, ...), condition=%wide.region_18.19_spmd.clone, body=%wide.region_6.18_spmd.clone.sunk | while | flops 692868864 | bytes 118107712 | solution.py:206
  112.7 3.8 fusion.345
  116.6 5.5 multiply_multiply_fusion.19
  129.5 2.7 fusion.348
  132.2 3.6 multiply_reduce_fusion.13
  158.6 3.8 fusion.345
  162.5 5.5 multiply_multiply_fusion.19
  175.4 2.7 fusion.348
  178.0 3.6 multiply_reduce_fusion.13
  196.5 1.9 bitcast_add_fusion.2
  205.6 3.8 fusion.345
  209.4 5.5 multiply_multiply_fusion.19
  222.3 2.7 fusion.348
  225.0 3.6 multiply_reduce_fusion.13
  243.5 1.9 bitcast_add_fusion.2
  252.5 3.8 fusion.345
  256.3 5.5 multiply_multiply_fusion.19
  269.3 2.7 fusion.348
  271.9 3.6 multiply_reduce_fusion.13
  290.4 1.9 bitcast_add_fusion.2
  299.4 3.8 fusion.345
  303.3 5.5 multiply_multiply_fusion.19
  316.2 2.7 fusion.348
  318.9 3.6 multiply_reduce_fusion.13
  337.4 1.9 bitcast_add_fusion.2
  346.4 3.8 fusion.345
  350.2 5.5 multiply_multiply_fusion.19
  363.2 2.7 fusion.348
  365.8 3.6 multiply_reduce_fusion.13
  384.3 1.9 bitcast_add_fusion.2
  393.3 3.8 fusion.345
  397.2 5.5 multiply_multiply_fusion.19
  410.1 2.7 fusion.348
  412.8 3.6 multiply_reduce_fusion.13
  440.3 3.8 fusion.345
  444.1 5.5 multiply_multiply_fusion.19
  457.0 2.7 fusion.348
  459.7 3.6 multiply_reduce_fusion.13
  481.2 10.9 %psum.7 = f32[32,256]{1,0:T(8,128)S(1)} all-reduce(f32[32,256]{1,0:T(8,128)S(1)} %reshape.333), channel_id=1, replica_groups=mesh['groups'=2,'prompt'=4,'enc'=4] {'enc'}, use_global_device_ids=true, to_apply=%region_19.20 | all-reduce | flops 8192 | bytes 65536 | tf_op jit(solution)/shard_map/psum | solution.py:210
  496.0 2.1 fusion.118
  504.4 82.4 %all-gather.8.cloned.1.call-done = f32[4096,256]{1,0:T(8,128)} async-done(((f32[1024,256]{1,0:T(8,128)}), f32[4096,256]{1,0:T(8,128)}) %all-gather.8.cloned.1.call-update) | async-done | bytes 4194320 | tf_op jit(solution)/shard_map/all_gather | solution.py:136
  586.7 2.6 reduce_sum.175
  (1285 shorter events, 256.2 us)
Async XLA Ops:
  6.5 98.0 %copy-start = (bf16[256,128]{1,0:T(8,128)(2,1)S(1)}, bf16[256,128]{1,0:T(8,128)(2,1)}, u32[]{:S(2)}) copy-start(bf16[256,128]{1,0:T(8,128)(2,1)} %param.37) | copy-start | bytes 196612
  6.5 23.2 %copy-start.57 = (bf16[256,128]{1,0:T(8,128)(2,1)S(1)}, bf16[256,128]{1,0:T(8,128)(2,1)}, u32[]{:S(2)}) copy-start(bf16[256,128]{1,0:T(8,128)(2,1)} %param.34) | copy-start | bytes 196612
  6.5 23.5 %copy-start.59 = (bf16[256,128]{1,0:T(8,128)(2,1)S(1)}, bf16[256,128]{1,0:T(8,128)(2,1)}, u32[]{:S(2)}) copy-start(bf16[256,128]{1,0:T(8,128)(2,1)} %param.35) | copy-start | bytes 196612
  6.5 580.2 %all-gather.8.cloned.1.call-start = ((), (), s32[]{:S(2)}) async-start(), calls=%async_computation | async-start | bytes 5242880 | tf_op jit(solution)/shard_map/all_gather | solution.py:136
  33.8 18.3 %copy-start.56 = (bf16[128,256]{1,0:T(8,128)(2,1)S(1)}, bf16[128,256]{1,0:T(8,128)(2,1)}, u32[]{:S(2)}) copy-start(bf16[128,256]{1,0:T(8,128)(2,1)} %param.36) | copy-start | bytes 196612
  33.8 19.2 %copy-start.70 = (f32[256]{0:T(256)S(1)}, f32[256]{0:T(256)}, u32[]{:S(2)}) copy-start(f32[256]{0:T(256)} %param.41) | copy-start | bytes 3076
  33.8 19.9 %copy-start.74 = (s32[4]{0:T(128)S(1)}, s32[4]{0:T(128)}, u32[]{:S(2)}) copy-start(s32[4]{0:T(128)} %param.29) | copy-start | bytes 52
  33.8 21.6 %copy-start.55 = (s32[256,256]{1,0:T(8,128)S(1)}, s32[256,256]{1,0:T(8,128)}, u32[]{:S(2)}) copy-start(s32[256,256]{1,0:T(8,128)} %param.30) | copy-start | bytes 786436
  52.0 30.4 %copy-start.63 = (f32[32,8]{0,1:T(8,128)}, f32[32,8]{0,1:T(8,128)S(1)}, u32[]{:S(2)}) copy-start(f32[32,8]{0,1:T(8,128)S(1)} %get-tuple-element.283) | copy-start | bytes 3076
  52.0 30.4 %copy-start.65 = (f32[32,8]{0,1:T(8,128)}, f32[32,8]{0,1:T(8,128)S(1)}, u32[]{:S(2)}) copy-start(f32[32,8]{0,1:T(8,128)S(1)} %get-tuple-element.286) | copy-start | bytes 3076
  52.0 30.4 %copy-start.52 = (f32[32,8,16]{0,2,1:T(8,128)}, f32[32,8,16]{0,2,1:T(8,128)S(1)}, u32[]{:S(2)}) copy-start(f32[32,8,16]{0,2,1:T(8,128)S(1)} %broadcast_divide_fusion) | copy-start | bytes 49156
  52.4 30.0 %copy-start.71 = (f32[32]{0:T(128)}, f32[32]{0:T(128)S(1)}, u32[]{:S(2)}) copy-start(f32[32]{0:T(128)S(1)} %broadcast_multiply_fusion.3) | copy-start | bytes 388
  52.6 29.8 %copy-start.73 = (f32[32]{0:T(128)}, f32[32]{0:T(128)S(1)}, u32[]{:S(2)}) copy-start(f32[32]{0:T(128)S(1)} %multiply_reduce_fusion.6) | copy-start | bytes 388
  53.0 29.5 %copy-start.72 = (f32[32]{0:T(128)}, f32[32]{0:T(128)S(1)}, u32[]{:S(2)}) copy-start(f32[32]{0:T(128)S(1)} %fusion.146) | copy-start | bytes 388
  105.7 5.0 copy-start.22
  116.5 5.6 copy-start.5
  116.5 5.6 copy-start.18
  116.5 6.4 %copy-start.53 = (bf16[256,32]{0,1:T(8,128)(2,1)S(1)}, bf16[256,32]{0,1:T(8,128)(2,1)}, u32[]{:S(2)}) copy-start(bf16[256,32]{0,1:T(8,128)(2,1)} %get-tuple-element.825) | copy-start | bytes 49156 | tf_op jit(solution)/shard_map/while
  141.7 6.0 %copy-start.4 = (f32[1024,256]{0,1:T(8,128)S(1)}, f32[1024,256]{0,1:T(8,128)}, u32[]{:S(2)}) copy-start(f32[1024,256]{0,1:T(8,128)} %copy-done.3) | copy-start | bytes 3145732 | tf_op jit(solution)/shard_map/while
  162.4 5.6 copy-start.5
  162.4 5.6 copy-start.18
  162.4 6.4 %copy-start.53 = (bf16[256,32]{0,1:T(8,128)(2,1)S(1)}, bf16[256,32]{0,1:T(8,128)(2,1)}, u32[]{:S(2)}) copy-start(bf16[256,32]{0,1:T(8,128)(2,1)} %get-tuple-element.825) | copy-start | bytes 49156 | tf_op jit(solution)/shard_map/while
  187.5 6.0 %copy-start.4 = (f32[1024,256]{0,1:T(8,128)S(1)}, f32[1024,256]{0,1:T(8,128)}, u32[]{:S(2)}) copy-start(f32[1024,256]{0,1:T(8,128)} %copy-done.3) | copy-start | bytes 3145732 | tf_op jit(solution)/shard_map/while
  209.4 5.6 copy-start.5
  209.4 5.6 copy-start.18
  209.4 6.5 %copy-start.53 = (bf16[256,32]{0,1:T(8,128)(2,1)S(1)}, bf16[256,32]{0,1:T(8,128)(2,1)}, u32[]{:S(2)}) copy-start(bf16[256,32]{0,1:T(8,128)(2,1)} %get-tuple-element.825) | copy-start | bytes 49156 | tf_op jit(solution)/shard_map/while
  234.5 6.0 %copy-start.4 = (f32[1024,256]{0,1:T(8,128)S(1)}, f32[1024,256]{0,1:T(8,128)}, u32[]{:S(2)}) copy-start(f32[1024,256]{0,1:T(8,128)} %copy-done.3) | copy-start | bytes 3145732 | tf_op jit(solution)/shard_map/while
  256.3 5.6 copy-start.5
  256.3 5.6 copy-start.18
  256.3 6.5 %copy-start.53 = (bf16[256,32]{0,1:T(8,128)(2,1)S(1)}, bf16[256,32]{0,1:T(8,128)(2,1)}, u32[]{:S(2)}) copy-start(bf16[256,32]{0,1:T(8,128)(2,1)} %get-tuple-element.825) | copy-start | bytes 49156 | tf_op jit(solution)/shard_map/while
  281.5 6.0 %copy-start.4 = (f32[1024,256]{0,1:T(8,128)S(1)}, f32[1024,256]{0,1:T(8,128)}, u32[]{:S(2)}) copy-start(f32[1024,256]{0,1:T(8,128)} %copy-done.3) | copy-start | bytes 3145732 | tf_op jit(solution)/shard_map/while
  303.3 5.6 copy-start.5
  303.3 5.6 copy-start.18
  303.3 6.5 %copy-start.53 = (bf16[256,32]{0,1:T(8,128)(2,1)S(1)}, bf16[256,32]{0,1:T(8,128)(2,1)}, u32[]{:S(2)}) copy-start(bf16[256,32]{0,1:T(8,128)(2,1)} %get-tuple-element.825) | copy-start | bytes 49156 | tf_op jit(solution)/shard_map/while
  328.4 6.0 %copy-start.4 = (f32[1024,256]{0,1:T(8,128)S(1)}, f32[1024,256]{0,1:T(8,128)}, u32[]{:S(2)}) copy-start(f32[1024,256]{0,1:T(8,128)} %copy-done.3) | copy-start | bytes 3145732 | tf_op jit(solution)/shard_map/while
  339.3 4.9 copy-start.7
  350.2 5.6 copy-start.5
  350.2 5.6 copy-start.18
  350.2 6.5 %copy-start.53 = (bf16[256,32]{0,1:T(8,128)(2,1)S(1)}, bf16[256,32]{0,1:T(8,128)(2,1)}, u32[]{:S(2)}) copy-start(bf16[256,32]{0,1:T(8,128)(2,1)} %get-tuple-element.825) | copy-start | bytes 49156 | tf_op jit(solution)/shard_map/while
  375.3 6.0 %copy-start.4 = (f32[1024,256]{0,1:T(8,128)S(1)}, f32[1024,256]{0,1:T(8,128)}, u32[]{:S(2)}) copy-start(f32[1024,256]{0,1:T(8,128)} %copy-done.3) | copy-start | bytes 3145732 | tf_op jit(solution)/shard_map/while
  397.2 5.6 copy-start.5
  397.2 5.6 copy-start.18
  397.2 6.4 %copy-start.53 = (bf16[256,32]{0,1:T(8,128)(2,1)S(1)}, bf16[256,32]{0,1:T(8,128)(2,1)}, u32[]{:S(2)}) copy-start(bf16[256,32]{0,1:T(8,128)(2,1)} %get-tuple-element.825) | copy-start | bytes 49156 | tf_op jit(solution)/shard_map/while
  422.3 6.0 %copy-start.4 = (f32[1024,256]{0,1:T(8,128)S(1)}, f32[1024,256]{0,1:T(8,128)}, u32[]{:S(2)}) copy-start(f32[1024,256]{0,1:T(8,128)} %copy-done.3) | copy-start | bytes 3145732 | tf_op jit(solution)/shard_map/while
  444.1 5.6 copy-start.5
  444.1 5.6 copy-start.18
  444.1 6.4 %copy-start.53 = (bf16[256,32]{0,1:T(8,128)(2,1)S(1)}, bf16[256,32]{0,1:T(8,128)(2,1)}, u32[]{:S(2)}) copy-start(bf16[256,32]{0,1:T(8,128)(2,1)} %get-tuple-element.825) | copy-start | bytes 49156 | tf_op jit(solution)/shard_map/while
  469.2 6.0 %copy-start.4 = (f32[1024,256]{0,1:T(8,128)S(1)}, f32[1024,256]{0,1:T(8,128)}, u32[]{:S(2)}) copy-start(f32[1024,256]{0,1:T(8,128)} %copy-done.3) | copy-start | bytes 3145732 | tf_op jit(solution)/shard_map/while
  (373 other events, 937.8 us)
Sparse Core Ops, SparseCore 0:
  504.5 82.2 all-gather.7
